TPU v7x, 256 devices: a whole 4x4x8 slice. The times are simulated.
256 devices in a mesh: pipe: 8 (over z_hi, x), expert: 32 (over y, z_lo, core).
Axes of the slice: x: 4, y: 4, z: 8 (z_hi: 2, z_lo: 4; z = z_hi * 4 + z_lo), core: 2. Of those that a mesh axis runs over, the one named last changes fastest.
Arguments:
- grad_out: bfloat16 [8, 4096, 2048], P('pipe', 'expert'), may hold values from -6 to 6
- expert_ids: int32 [8, 4096, 8], P('pipe', 'expert'), may hold values from 0 to 63, as said below
- slot_ids: int32 [8, 4096, 8], P('pipe', 'expert'), may hold values from 0 to 16, as said below
- gate_weights: float32 [8, 4096, 8], P('pipe', 'expert'), may hold values from 0.02 to 0.6
- saved_pre: bfloat16 [8, 64, 512, 1536], P('pipe', 'expert'), may hold values from -6 to 6
- down_weight: bfloat16 [8, 64, 768, 2048], P('pipe', 'expert'), may hold values from -0.21875 to 0.21875
- router_weight: bfloat16 [8, 64, 2048], P('pipe', 'expert'), may hold values from -0.125 to 0.125
Outputs:
- pre_grad: bfloat16 [8, 64, 512, 1536], P('pipe', 'expert')
- grad_inputs: bfloat16 [8, 4096, 2048], P('pipe', 'expert')
Inputs may be any that keep to these rules, and one draw needn't show every extreme that they name: `expert_ids`: each row names 8 different experts. `slot_ids`: for the pair (t, k): the number of earlier pairs (by row, then by k) among the same device's 128 rows of that section that name the same expert, capped at 16; the value 16 marks a pair that is dropped.
All inputs are finite; a program needn't handle non-finite values.
Results may differ from a plain program's by a relative error of at most 0.012.
Values may be sent and summed in bfloat16 or wider, within the bound.
No kernel may reach another device: no remote copies, remote signals or barrier semaphores. Data moves between devices by JAX's collectives and lax.ppermute only.
A program may use at most 128 MiB of HBM per device.

v0:
```python
import jax
import jax.numpy as jnp
from jax import lax
from jax.sharding import PartitionSpec as P


def passed_along(value, axis, by):
    peers = lax.axis_size(axis)
    return lax.ppermute(value, axis, [(i, (i + by) % peers) for i in range(peers)])


def per_device(grad_out, expert_ids, slot_ids, gate_weights, saved_pre, down_weight, router_weight):
    groups = lax.axis_size("expert")
    local_experts = down_weight.shape[1]
    hidden_width = down_weight.shape[2]
    tok_rows = grad_out.shape[1]
    top_count = expert_ids.shape[2]
    expert_total = local_experts * groups
    capacity = tok_rows * top_count // expert_total
    total_rows = expert_total * capacity
    features = grad_out[0]
    route_ids = expert_ids[0]
    kept_pairs = slot_ids[0] < capacity
    destination = (
        route_ids % local_experts * (groups * capacity)
        + route_ids // local_experts * capacity
        + jnp.minimum(slot_ids[0], capacity - 1)
    )
    pair_dest = jnp.where(kept_pairs, destination, total_rows).reshape(-1)
    row_ids = jnp.arange(total_rows, dtype=jnp.int32)
    matches = pair_dest[None, :] == row_ids[:, None]
    pair_token = jnp.arange(tok_rows * top_count, dtype=jnp.int32) // top_count
    slot_token = jnp.sum(jnp.where(matches, pair_token[None, :], 0), axis=1)
    occupied = jnp.any(matches, axis=1)
    gate_low = gate_weights[0].astype(jnp.bfloat16)
    slot_gate = jnp.sum(
        jnp.where(matches, gate_low.reshape(-1).astype(jnp.float32)[None, :], jnp.float32(0.0)),
        axis=1,
    )
    token_rows = jnp.take(features, slot_token, axis=0)
    token_rows = jnp.where(occupied[:, None], token_rows, jnp.zeros_like(token_rows))
    pre_saved = saved_pre[0]
    gate_part = pre_saved[..., :hidden_width].astype(jnp.float32)
    up_part = pre_saved[..., hidden_width:].astype(jnp.float32)
    sigmoid_gate = jax.nn.sigmoid(gate_part)
    silu_gate = gate_part * sigmoid_gate
    hidden = (silu_gate * up_part).astype(jnp.bfloat16)
    weights = down_weight[0]
    expert_out = jnp.einsum(
        "jsf,jfd->jsd", hidden, weights, preferred_element_type=jnp.float32
    ).astype(jnp.bfloat16)
    scaled = (slot_gate[:, None] * token_rows.astype(jnp.float32)).astype(jnp.bfloat16)
    arrived = lax.all_to_all(
        scaled.reshape(local_experts, groups, capacity, -1),
        "expert",
        split_axis=1,
        concat_axis=1,
        tiled=True,
    )
    scaled_rows = arrived.reshape(local_experts, groups * capacity, -1)
    returned = lax.all_to_all(
        expert_out.reshape(local_experts, groups, capacity, -1),
        "expert",
        split_axis=1,
        concat_axis=1,
        tiled=True,
    )
    pair_out = jnp.take(
        returned.reshape(total_rows, -1), pair_dest, axis=0, mode="fill", fill_value=0
    )
    pair_scores = jnp.sum(
        pair_out.reshape(tok_rows, top_count, -1).astype(jnp.float32)
        * features.astype(jnp.float32)[:, None, :],
        axis=-1,
    )
    row_grad = jnp.einsum("jsd,jfd->jsf", scaled_rows, weights, preferred_element_type=jnp.float32)
    gate_grad = row_grad * up_part * sigmoid_gate * (1.0 + gate_part * (1.0 - sigmoid_gate))
    up_grad = row_grad * silu_gate
    pre_grad = jnp.concatenate([gate_grad, up_grad], axis=-1).astype(jnp.bfloat16)
    gate_values = gate_weights[0]
    weighted_sum = jnp.sum(gate_values * pair_scores, axis=-1, keepdims=True)
    select_grad = gate_values * (pair_scores - weighted_sum)
    expert_columns = jnp.arange(expert_total, dtype=jnp.int32)
    chosen = route_ids[:, :, None] == expert_columns[None, None, :]
    logit_grad = jnp.sum(
        jnp.where(chosen, select_grad[:, :, None], jnp.float32(0.0)), axis=1
    ).astype(jnp.bfloat16)
    router_part = jnp.dot(
        logit_grad,
        lax.all_gather(router_weight[0], "expert", axis=0, tiled=True),
        preferred_element_type=jnp.float32,
    )
    section_grad = (features.astype(jnp.float32) + router_part).astype(jnp.bfloat16)
    outgoing = passed_along(section_grad, "pipe", -1)
    return (pre_grad[None], outgoing[None])


def solution(mesh):
    in_specs = (
        P("pipe", "expert", None),
        P("pipe", "expert", None),
        P("pipe", "expert", None),
        P("pipe", "expert", None),
        P("pipe", "expert", None, None),
        P("pipe", "expert", None, None),
        P("pipe", "expert", None),
    )
    out_specs = (P("pipe", "expert", None, None), P("pipe", "expert", None))
    return jax.shard_map(
        per_device, mesh=mesh, in_specs=in_specs, out_specs=out_specs, check_vma=False
    )
```

profile of v0, /device:TPU:7, one launch (start us, length us, event | category | flops | bytes accessed | tf_op | source)
XLA Modules:
  0.0 298.4 jit_solution(13683775158880791183)
XLA Ops:
  0.6 7.4 %fusion.7 = bf16[2,512,2048]{2,1,0:T(8,128)(2,1)S(1)} fusion(bf16[1,2,768,2048]{3,2,1,0:T(8,128)(2,1)} %param.12, bf16[2,512,1536]{2,1,0:T(8,128)(2,1)} %bitcast.59), kind=kOutput, calls=%fused_computation.20 | convolution fusion | flops 3229614080 | bytes 13631488 | tf_op jit(solution)/shard_map/jsf,jfd->jsd/dot_general | solution.py:49
  8.0 2.3 copy.68
  10.3 9.6 %all-to-all-start.1 = ((bf16[2,32,16,2048]{3,2,0,1:T(8,128)(2,1)}), bf16[2,32,16,2048]{3,2,0,1:T(8,128)(2,1)}, u32[]{:S(2)}, u32[]{:S(2)}) async-start(bf16[2,32,16,2048]{3,2,0,1:T(8,128)(2,1)} %copy.68), calls=%async_computation.1 | async-start | bytes 8388608 | tf_op jit(solution)/shard_map/all_to_all | solution.py:61
  20.0 0.1 copy.57
  20.5 0.5 select_reduce_fusion
  21.4 0.5 select_reduce_fusion.1
  22.0 0.6 fusion.6
  22.7 6.0 %gather_fusion = bf16[1024,2048]{1,0:T(8,128)(2,1)} fusion(bf16[128,2048]{1,0:T(8,128)(2,1)S(1)} %bitcast.49, s32[1024]{0:T(1024)S(1)} %broadcast_clamp_fusion.1), kind=kCustom, calls=%fused_computation | custom fusion | bytes 8392704 | tf_op jit(solution)/shard_map/jit(_take)/gather | solution.py:40
  28.7 4.5 %multiply_convert_fusion = bf16[2,32,16,2048]{3,2,0,1:T(8,128)(2,1)} fusion(bf16[2,32,16,2048]{3,2,1,0:T(8,128)(2,1)} %bitcast.51, f32[2,32,16]{2,0,1:T(2,128)S(1)} %copy.61, pred[2,32,16]{2,0,1:T(4,128)(4,1)S(1)} %copy.63, pred[2,32,16]{2,0,1:T(4,128)(4,1)S(1)} %copy.62), kind=kLoop, calls=%fused_computation.4 | loop fusion | flops 10485760 | bytes 8394752 | tf_op jit(solution)/shard_map/convert_element_type | solution.py:52
  33.3 81.1 %all-to-all-done.1 = bf16[2,32,16,2048]{3,2,0,1:T(8,128)(2,1)} async-done(((bf16[2,32,16,2048]{3,2,0,1:T(8,128)(2,1)}), bf16[2,32,16,2048]{3,2,0,1:T(8,128)(2,1)}, u32[]{:S(2)}, u32[]{:S(2)}) %all-to-all-start.1) | async-done | bytes 4194336 | tf_op jit(solution)/shard_map/all_to_all | solution.py:61
  114.4 5.5 %all-to-all-start = ((bf16[2,32,16,2048]{3,2,0,1:T(8,128)(2,1)}), bf16[2,32,16,2048]{3,2,0,1:T(8,128)(2,1)}, u32[]{:S(2)}, u32[]{:S(2)}) async-start(bf16[2,32,16,2048]{3,2,0,1:T(8,128)(2,1)} %multiply_convert_fusion), calls=%async_computation | async-start | bytes 8388608 | tf_op jit(solution)/shard_map/all_to_all | solution.py:53
  120.3 0.1 copy.67
  120.6 126.3 %all-gather = bf16[1,64,2048]{2,0,1:T(2,128)(2,1)S(1)} all-gather(bf16[1,2,2048]{2,0,1:T(2,128)(2,1)S(1)} %copy.74), channel_id=2, replica_groups=mesh['pipe'=8,'expert'=32] {'expert'}, dimensions={1}, use_global_device_ids=true | all-gather | bytes 270336 | tf_op jit(solution)/shard_map/all_gather | solution.py:90
  247.0 4.7 %copy.69 = bf16[2,32,16,2048]{3,2,1,0:T(8,128)(2,1)} copy(bf16[2,32,16,2048]{3,2,0,1:T(8,128)(2,1)} %all-to-all-done.1) | data formatting | bytes 8388608 | tf_op jit(solution)/shard_map/all_to_all | solution.py:61
  251.8 11.6 %gather_fusion.1 = bf16[1024,2048]{1,0:T(8,128)(2,1)} fusion(bf16[1024,2048]{1,0:T(8,128)(2,1)} %bitcast.50, s32[1024]{0:T(1024)S(1)} %broadcast_clamp_fusion), kind=kCustom, calls=%fused_computation.1 | custom fusion | bytes 8392704 | tf_op jit(solution)/shard_map/jit(_take)/gather | solution.py:68
  263.3 3.2 %fusion = f32[1024]{0:T(1024)S(1)} fusion(f32[128,2048]{1,0:T(8,128)S(1)} %bitcast_convert_fusion, bf16[1024,2048]{1,0:T(8,128)(2,1)} %gather_fusion.1, pred[1024]{0:T(1024)(128)(4,1)S(1)} %broadcast_in_dim.103), kind=kLoop, calls=%fused_computation.3 | loop fusion | flops 8387584 | bytes 5248000 | tf_op jit(solution)/shard_map/reduce_sum | solution.py:71
  267.0 0.3 fusion.18
  267.3 0.8 collective-permute-start
  268.1 2.7 copy.65
  270.8 0.5 copy-done.5
  271.3 7.3 %fusion.21 = (bf16[1,2,512,768]{3,2,1,0:T(8,128)(2,1)S(1)}, bf16[1,2,512,768]{3,2,1,0:T(8,128)(2,1)S(1)}) fusion(bf16[2,512,1536]{2,1,0:T(8,128)(2,1)S(1)} %bitcast.60, bf16[2,512,2048]{2,1,0:T(8,128)(2,1)S(1)} %bitcast.52, bf16[1,2,768,2048]{3,2,1,0:T(8,128)(2,1)} %param.12), kind=kOutput, calls=%fused_computation.34 | convolution fusion | flops 3233021952 | bytes 16777216 | tf_op jit(solution)/shard_map/jsd,jfd->jsf/dot_general | solution.py:76
  278.5 1.9 pad_maximum_fusion
  280.5 17.2 %collective-permute-done = bf16[128,2048]{1,0:T(8,128)(2,1)S(1)} collective-permute-done((bf16[128,2048]{1,0:T(8,128)(2,1)S(1)}, bf16[128,2048]{1,0:T(8,128)(2,1)S(1)}, u32[]{:S(2)}, u32[]{:S(2)}) %collective-permute-start) | collective-permute-done | bytes 524320 | tf_op jit(solution)/shard_map/ppermute | solution.py:9
  297.6 0.8 copy.86
  (46 shorter events, 2.1 us)
Async XLA Ops:
  10.3 9.6 %copy-start.1 = (s32[1,128,8]{1,2,0:T(8,128)S(1)}, s32[1,128,8]{1,2,0:T(8,128)}, u32[]{:S(2)}) copy-start(s32[1,128,8]{1,2,0:T(8,128)} %param.8) | copy-start | bytes 12292
  10.3 9.7 %copy-start.3 = (s32[1,128,8]{1,2,0:T(8,128)S(1)}, s32[1,128,8]{1,2,0:T(8,128)}, u32[]{:S(2)}) copy-start(s32[1,128,8]{1,2,0:T(8,128)} %param.9) | copy-start | bytes 12292
  10.3 10.9 %copy-start.2 = (f32[1,128,8]{1,2,0:T(8,128)S(1)}, f32[1,128,8]{1,2,0:T(8,128)}, u32[]{:S(2)}) copy-start(f32[1,128,8]{1,2,0:T(8,128)} %param.10) | copy-start | bytes 12292
  10.3 12.4 %copy-start = (bf16[1,128,2048]{2,1,0:T(8,128)(2,1)S(1)}, bf16[1,128,2048]{2,1,0:T(8,128)(2,1)}, u32[]{:S(2)}) copy-start(bf16[1,128,2048]{2,1,0:T(8,128)(2,1)} %param.7) | copy-start | bytes 1572868
  10.3 104.1 %all-to-all-start.1 = ((bf16[2,32,16,2048]{3,2,0,1:T(8,128)(2,1)}), bf16[2,32,16,2048]{3,2,0,1:T(8,128)(2,1)}, u32[]{:S(2)}, u32[]{:S(2)}) async-start(bf16[2,32,16,2048]{3,2,0,1:T(8,128)(2,1)} %copy.68), calls=%async_computation.1 | async-start | bytes 8388608 | tf_op jit(solution)/shard_map/all_to_all | solution.py:61
  33.3 87.3 %copy-start.4 = (bf16[1,2,2048]{2,1,0:T(2,128)(2,1)S(1)}, bf16[1,2,2048]{2,1,0:T(2,128)(2,1)}, u32[]{:S(2)}) copy-start(bf16[1,2,2048]{2,1,0:T(2,128)(2,1)} %param.13) | copy-start | bytes 24580
  114.4 153.7 %all-to-all-start = ((bf16[2,32,16,2048]{3,2,0,1:T(8,128)(2,1)}), bf16[2,32,16,2048]{3,2,0,1:T(8,128)(2,1)}, u32[]{:S(2)}, u32[]{:S(2)}) async-start(bf16[2,32,16,2048]{3,2,0,1:T(8,128)(2,1)} %multiply_convert_fusion), calls=%async_computation | async-start | bytes 8388608 | tf_op jit(solution)/shard_map/all_to_all | solution.py:53
  267.3 30.3 %collective-permute-start = (bf16[128,2048]{1,0:T(8,128)(2,1)S(1)}, bf16[128,2048]{1,0:T(8,128)(2,1)S(1)}, u32[]{:S(2)}, u32[]{:S(2)}) collective-permute-start(bf16[128,2048]{1,0:T(8,128)(2,1)S(1)} %fusion.18), channel_id=1, source_target_pairs={{0,224},{32,0},{64,32},{96,64},{128,96},{160,128},{192,160},{224,1... | collective-permute-start | bytes 1572872 | tf_op jit(solution)/shard_map/ppermute | solution.py:9
  268.1 3.2 %copy-start.5 = (bf16[1,2,512,1536]{3,2,1,0:T(8,128)(2,1)S(1)}, bf16[1,2,512,1536]{3,2,1,0:T(8,128)(2,1)}, u32[]{:S(2)}) copy-start(bf16[1,2,512,1536]{3,2,1,0:T(8,128)(2,1)} %param.11) | copy-start | bytes 9437188
where the time goes:
time: 299 us; the launch traced here: 298 us
  blocking collectives  126 us (42%)
  waiting for transfers between devices  98.3 us (33%)
  local copies, waits for them, and re-layouts  30.4 us (10%)
  starting transfers between devices  15.9 us (5%)
  matrix products  15 us (5%)
  other arithmetic  11.7 us (4%)
    all_gather x1, blocking collectives, per_device(): lax.all_gather(router_weight[0], 'expert', axis=0, tiled=True)  126 us
    all_to_all x1, waiting for transfers between devices, per_device(): lax.all_to_all(expert_out.reshape(local_experts, groups, capacity, -1), '...  81.1 us
    ppermute x1, waiting for transfers between devices, passed_along(): lax.ppermute(value, axis, [(i, (i + by) % peers) for i in range(peers)])  17.2 us
    gather x1, local copies, waits for them, and re-layouts, per_device(): jnp.take(returned.reshape(total_rows, -1), pair_dest, axis=0, mode='fill'...  11.6 us
    all_to_all x1, starting transfers between devices, per_device(): lax.all_to_all(expert_out.reshape(local_experts, groups, capacity, -1), '...  9.56 us
    dot_general x1, matrix products, per_device(): jnp.einsum('jsf,jfd->jsd', hidden, weights, preferred_element_type=jnp.fl...  7.37 us
    dot_general x1, matrix products, per_device(): jnp.einsum('jsd,jfd->jsf', scaled_rows, weights, preferred_element_type=j...  7.27 us
    gather x1, local copies, waits for them, and re-layouts, per_device(): token_rows = jnp.take(features, slot_token, axis=0)  6.02 us
  transfers between devices with their start and end apart: 3, of which 2 were waited for; matrix products, arithmetic and copies ran while one was open for 15% of the time, Pallas kernels for 0%

commit v1 on v0

--- a/solution.py
+++ b/solution.py
@@ -87,7 +87,10 @@
     ).astype(jnp.bfloat16)
     router_part = jnp.dot(
         logit_grad,
-        lax.all_gather(router_weight[0], "expert", axis=0, tiled=True),
+        jnp.concatenate(
+            lax.all_to_all(jnp.stack([router_weight[0]] * lax.axis_size("expert")), "expert", 0, 0),
+            axis=0,
+        ),
         preferred_element_type=jnp.float32,
     )
     section_grad = (features.astype(jnp.float32) + router_part).astype(jnp.bfloat16)

time: 299 us -> 261 us (0.87)
  the two profiles are of different devices: /device:TPU:7 before, /device:TPU:1 now
where the time goes in v1:
time: 261 us; the launch traced here: 260 us
  waiting for transfers between devices  172 us (66%)
  local copies, waits for them, and re-layouts  32 us (12%)
  starting transfers between devices  28.6 us (11%)
  matrix products  15 us (6%)
  other arithmetic  11.7 us (4%)
    all_to_all x1, waiting for transfers between devices, per_device(): lax.all_to_all(scaled.reshape(local_experts, groups, capacity, -1), 'expe...  89.2 us
    all_to_all x1, waiting for transfers between devices, per_device(): lax.all_to_all(expert_out.reshape(local_experts, groups, capacity, -1), '...  81.1 us
    gather x1, local copies, waits for them, and re-layouts, per_device(): jnp.take(returned.reshape(total_rows, -1), pair_dest, axis=0, mode='fill'...  11.6 us
    all_to_all x1, starting transfers between devices, per_device(): lax.all_to_all(jnp.stack([router_weight[0]] * lax.axis_size('expert')), '...  10.2 us
    dot_general x1, matrix products, per_device(): jnp.einsum('jsf,jfd->jsd', hidden, weights, preferred_element_type=jnp.fl...  7.37 us
    dot_general x1, matrix products, per_device(): jnp.einsum('jsd,jfd->jsf', scaled_rows, weights, preferred_element_type=j...  7.27 us
    ppermute x1, starting transfers between devices, passed_along(): lax.ppermute(value, axis, [(i, (i + by) % peers) for i in range(peers)])  6.66 us
    all_to_all x1, starting transfers between devices, per_device(): lax.all_to_all(expert_out.reshape(local_experts, groups, capacity, -1), '...  6.31 us
  transfers between devices with their start and end apart: 4, of which 3 were waited for; matrix products, arithmetic and copies ran while one was open for 21% of the time, Pallas kernels for 0%

profile of v1, /device:TPU:1, one launch (start us, length us, event | category | flops | bytes accessed | tf_op | source)
XLA Modules:
  0.0 260.1 jit_solution(5292674042120520201)
XLA Ops:
  0.6 1.5 stack.3
  2.2 10.2 %all-to-all-start.2 = ((bf16[32,2,2048]{2,1,0:T(2,128)(2,1)}), bf16[32,2,2048]{2,1,0:T(2,128)(2,1)S(1)}, u32[]{:S(2)}, u32[]{:S(2)}) async-start(bf16[32,2,2048]{2,1,0:T(2,128)(2,1)} %stack.3), calls=%async_computation.2 | async-start | bytes 524288 | tf_op jit(solution)/shard_map/all_to_all | solution.py:91
  12.4 7.4 %fusion.7 = bf16[2,512,2048]{2,1,0:T(8,128)(2,1)S(1)} fusion(bf16[1,2,768,2048]{3,2,1,0:T(8,128)(2,1)} %param.12, bf16[2,512,1536]{2,1,0:T(8,128)(2,1)} %bitcast.59), kind=kOutput, calls=%fused_computation.20 | convolution fusion | flops 3229614080 | bytes 13631488 | tf_op jit(solution)/shard_map/jsf,jfd->jsd/dot_general | solution.py:49
  19.7 2.3 copy.49
  22.0 1.6 all-to-all-done.2
  23.6 6.3 %all-to-all-start.1 = ((bf16[2,32,16,2048]{3,2,0,1:T(8,128)(2,1)}), bf16[2,32,16,2048]{3,2,0,1:T(8,128)(2,1)}, u32[]{:S(2)}, u32[]{:S(2)}) async-start(bf16[2,32,16,2048]{3,2,0,1:T(8,128)(2,1)} %copy.49), calls=%async_computation.1 | async-start | bytes 8388608 | tf_op jit(solution)/shard_map/all_to_all | solution.py:61
  30.6 0.5 select_reduce_fusion
  31.4 0.5 select_reduce_fusion.1
  32.1 0.6 fusion.6
  32.8 6.0 %gather_fusion = bf16[1024,2048]{1,0:T(8,128)(2,1)} fusion(bf16[128,2048]{1,0:T(8,128)(2,1)S(1)} %bitcast.48, s32[1024]{0:T(1024)S(1)} %broadcast_clamp_fusion.1), kind=kCustom, calls=%fused_computation | custom fusion | bytes 8392704 | tf_op jit(solution)/shard_map/jit(_take)/gather | solution.py:40
  38.8 4.5 %multiply_convert_fusion = bf16[2,32,16,2048]{3,2,0,1:T(8,128)(2,1)} fusion(bf16[2,32,16,2048]{3,2,1,0:T(8,128)(2,1)} %bitcast.50, f32[2,32,16]{2,0,1:T(2,128)S(1)} %copy.42, pred[2,32,16]{2,0,1:T(4,128)(4,1)S(1)} %copy.44, pred[2,32,16]{2,0,1:T(4,128)(4,1)S(1)} %copy.43), kind=kLoop, calls=%fused_computation.4 | loop fusion | flops 10485760 | bytes 8394752 | tf_op jit(solution)/shard_map/convert_element_type | solution.py:52
  43.3 81.1 %all-to-all-done.1 = bf16[2,32,16,2048]{3,2,0,1:T(8,128)(2,1)} async-done(((bf16[2,32,16,2048]{3,2,0,1:T(8,128)(2,1)}), bf16[2,32,16,2048]{3,2,0,1:T(8,128)(2,1)}, u32[]{:S(2)}, u32[]{:S(2)}) %all-to-all-start.1) | async-done | bytes 4194336 | tf_op jit(solution)/shard_map/all_to_all | solution.py:61
  124.4 5.5 %all-to-all-start = ((bf16[2,32,16,2048]{3,2,0,1:T(8,128)(2,1)}), bf16[2,32,16,2048]{3,2,0,1:T(8,128)(2,1)}, u32[]{:S(2)}, u32[]{:S(2)}) async-start(bf16[2,32,16,2048]{3,2,0,1:T(8,128)(2,1)} %multiply_convert_fusion), calls=%async_computation | async-start | bytes 8388608 | tf_op jit(solution)/shard_map/all_to_all | solution.py:53
  130.8 4.7 %copy.50 = bf16[2,32,16,2048]{3,2,1,0:T(8,128)(2,1)} copy(bf16[2,32,16,2048]{3,2,0,1:T(8,128)(2,1)} %all-to-all-done.1) | data formatting | bytes 8388608 | tf_op jit(solution)/shard_map/all_to_all | solution.py:61
  135.6 11.6 %gather_fusion.1 = bf16[1024,2048]{1,0:T(8,128)(2,1)} fusion(bf16[1024,2048]{1,0:T(8,128)(2,1)} %bitcast.49, s32[1024]{0:T(1024)S(1)} %broadcast_clamp_fusion), kind=kCustom, calls=%fused_computation.1 | custom fusion | bytes 8392704 | tf_op jit(solution)/shard_map/jit(_take)/gather | solution.py:68
  147.1 3.2 %fusion = f32[1024]{0:T(1024)S(1)} fusion(f32[128,2048]{1,0:T(8,128)S(1)} %bitcast_convert_fusion, bf16[1024,2048]{1,0:T(8,128)(2,1)} %gather_fusion.1, pred[1024]{0:T(1024)(128)(4,1)S(1)} %broadcast_in_dim.103), kind=kLoop, calls=%fused_computation.3 | loop fusion | flops 8387584 | bytes 5248000 | tf_op jit(solution)/shard_map/reduce_sum | solution.py:71
  150.8 0.3 fusion.18
  151.1 6.7 %collective-permute-start = (bf16[128,2048]{1,0:T(8,128)(2,1)S(1)}, bf16[128,2048]{1,0:T(8,128)(2,1)S(1)}, u32[]{:S(2)}, u32[]{:S(2)}) collective-permute-start(bf16[128,2048]{1,0:T(8,128)(2,1)S(1)} %fusion.18), channel_id=1, source_target_pairs={{0,224},{32,0},{64,32},{96,64},{128,96},{160,128},{192,160},{224,1... | collective-permute-start | bytes 1572872 | tf_op jit(solution)/shard_map/ppermute | solution.py:9
  157.8 89.2 %all-to-all-done = bf16[2,32,16,2048]{3,2,0,1:T(8,128)(2,1)} async-done(((bf16[2,32,16,2048]{3,2,0,1:T(8,128)(2,1)}), bf16[2,32,16,2048]{3,2,0,1:T(8,128)(2,1)}, u32[]{:S(2)}, u32[]{:S(2)}) %all-to-all-start) | async-done | bytes 4194336 | tf_op jit(solution)/shard_map/all_to_all | solution.py:53
  247.0 2.7 %copy.46 = bf16[2,32,16,2048]{3,2,1,0:T(8,128)(2,1)S(1)} copy(bf16[2,32,16,2048]{3,2,0,1:T(8,128)(2,1)} %all-to-all-done) | data formatting | bytes 8388608 | tf_op jit(solution)/shard_map/all_to_all | solution.py:53
  249.7 0.5 copy-done.4
  250.2 7.3 %fusion.21 = (bf16[1,2,512,768]{3,2,1,0:T(8,128)(2,1)S(1)}, bf16[1,2,512,768]{3,2,1,0:T(8,128)(2,1)S(1)}) fusion(bf16[2,512,1536]{2,1,0:T(8,128)(2,1)S(1)} %bitcast.60, bf16[2,512,2048]{2,1,0:T(8,128)(2,1)S(1)} %bitcast.51, bf16[1,2,768,2048]{3,2,1,0:T(8,128)(2,1)} %param.12), kind=kOutput, calls=%fused_computation.34 | convolution fusion | flops 3233021952 | bytes 16777216 | tf_op jit(solution)/shard_map/jsd,jfd->jsf/dot_general | solution.py:76
  257.4 1.9 pad_maximum_fusion
  259.3 0.8 copy.61
  (46 shorter events, 2.5 us)
Async XLA Ops:
  2.2 21.4 %all-to-all-start.2 = ((bf16[32,2,2048]{2,1,0:T(2,128)(2,1)}), bf16[32,2,2048]{2,1,0:T(2,128)(2,1)S(1)}, u32[]{:S(2)}, u32[]{:S(2)}) async-start(bf16[32,2,2048]{2,1,0:T(2,128)(2,1)} %stack.3), calls=%async_computation.2 | async-start | bytes 524288 | tf_op jit(solution)/shard_map/all_to_all | solution.py:91
  22.0 7.9 %copy-start.1 = (s32[1,128,8]{1,2,0:T(8,128)S(1)}, s32[1,128,8]{1,2,0:T(8,128)}, u32[]{:S(2)}) copy-start(s32[1,128,8]{1,2,0:T(8,128)} %param.8) | copy-start | bytes 12292
  22.0 8.0 %copy-start.3 = (s32[1,128,8]{1,2,0:T(8,128)S(1)}, s32[1,128,8]{1,2,0:T(8,128)}, u32[]{:S(2)}) copy-start(s32[1,128,8]{1,2,0:T(8,128)} %param.9) | copy-start | bytes 12292
  22.0 9.2 %copy-start.2 = (f32[1,128,8]{1,2,0:T(8,128)S(1)}, f32[1,128,8]{1,2,0:T(8,128)}, u32[]{:S(2)}) copy-start(f32[1,128,8]{1,2,0:T(8,128)} %param.10) | copy-start | bytes 12292
  22.0 10.7 %copy-start = (bf16[1,128,2048]{2,1,0:T(8,128)(2,1)S(1)}, bf16[1,128,2048]{2,1,0:T(8,128)(2,1)}, u32[]{:S(2)}) copy-start(bf16[1,128,2048]{2,1,0:T(8,128)(2,1)} %param.7) | copy-start | bytes 1572868
  23.6 100.8 %all-to-all-start.1 = ((bf16[2,32,16,2048]{3,2,0,1:T(8,128)(2,1)}), bf16[2,32,16,2048]{3,2,0,1:T(8,128)(2,1)}, u32[]{:S(2)}, u32[]{:S(2)}) async-start(bf16[2,32,16,2048]{3,2,0,1:T(8,128)(2,1)} %copy.49), calls=%async_computation.1 | async-start | bytes 8388608 | tf_op jit(solution)/shard_map/all_to_all | solution.py:61
  124.4 122.6 %all-to-all-start = ((bf16[2,32,16,2048]{3,2,0,1:T(8,128)(2,1)}), bf16[2,32,16,2048]{3,2,0,1:T(8,128)(2,1)}, u32[]{:S(2)}, u32[]{:S(2)}) async-start(bf16[2,32,16,2048]{3,2,0,1:T(8,128)(2,1)} %multiply_convert_fusion), calls=%async_computation | async-start | bytes 8388608 | tf_op jit(solution)/shard_map/all_to_all | solution.py:53
  151.1 108.2 %collective-permute-start = (bf16[128,2048]{1,0:T(8,128)(2,1)S(1)}, bf16[128,2048]{1,0:T(8,128)(2,1)S(1)}, u32[]{:S(2)}, u32[]{:S(2)}) collective-permute-start(bf16[128,2048]{1,0:T(8,128)(2,1)S(1)} %fusion.18), channel_id=1, source_target_pairs={{0,224},{32,0},{64,32},{96,64},{128,96},{160,128},{192,160},{224,1... | collective-permute-start | bytes 1572872 | tf_op jit(solution)/shard_map/ppermute | solution.py:9
  247.0 3.2 %copy-start.4 = (bf16[1,2,512,1536]{3,2,1,0:T(8,128)(2,1)S(1)}, bf16[1,2,512,1536]{3,2,1,0:T(8,128)(2,1)}, u32[]{:S(2)}) copy-start(bf16[1,2,512,1536]{3,2,1,0:T(8,128)(2,1)} %param.11) | copy-start | bytes 9437188
